TPU v7x, 32 devices: a whole 2x2x4 slice. The times are simulated.
32 devices in a mesh: snp: 8 (over z, y), ind: 4 (over x, core).
Axes of the slice: x: 2, y: 2, z: 4, core: 2. Of those that a mesh axis runs over, the one named last changes fastest.
Arguments:
- beta_hat: float32 [64, 8192], P('ind', 'snp'), may hold values from -8 to 8
- ld_band: float32 [8192, 1024], P('snp'), as said below
- band_start: int32 [64], P('snp'), may hold values from -480 to 7648, as said below
- heritability: float32 [64], P('ind'), may hold values from 0.2 to 0.6
- genotypes: bfloat16 [4096, 8192], P('ind', 'snp'), may hold values from 0 to 2, as said below
Outputs:
- weights: float32 [64, 8192], P('ind', 'snp')
- scores: float32 [64, 4096], P(None, ('ind', 'snp'))
Inputs may be any that keep to these rules, and one draw needn't show every extreme that they name: ld_band is a symmetric matrix R in band form: entry k of row i is R[i, band_start[i // 128] + k]; R[i, i] = 1; R[i, j] = 0 when |i - j| > 416 or j lies outside the SNPs; the off-diagonal magnitudes of a row sum to 2.5 at most. `band_start`: block b's window starts at 128 * b - 416 - k with k from 0 to 64; the first block has k = 64 and the last block k = 0. `genotypes`: dosages are 0, 1 or 2.
All inputs are finite; a program needn't handle non-finite values.
Results may differ from a plain program's by a relative error of at most 0.0021.
Values may be sent and summed in bfloat16 or wider, within the bound.
No kernel may reach another device: no remote copies, remote signals or barrier semaphores. Data moves between devices by JAX's collectives and lax.ppermute only.
A program may use at most 64 MiB of HBM per device.

v0:
```python
import jax
import jax.numpy as jnp
from jax import lax
from jax.sharding import PartitionSpec as P

BLK = 128
ITERS = 2
M_GENOME = 1100000
N_GWAS = 1000000
REACH = 416
SHIFT_BITS = 7


def all_sum(x, axes, count):
    sent = jnp.broadcast_to(x[None], (count,) + x.shape)
    return jnp.sum(lax.all_to_all(sent, axes, 0, 0, tiled=True), axis=0)


def with_halo(block, width):
    count = lax.axis_size("snp")
    forward = [(i, i + 1) for i in range(count - 1)]
    backward = [(target, source) for source, target in forward]
    low = lax.ppermute(block[:, block.shape[1] - width :], "snp", forward)
    high = lax.ppermute(block[:, :width], "snp", backward)
    return jnp.concatenate([low, block, high], axis=1)


def apply_operator(vector, ld_band, shifts, ridge_shift, halo):
    band_cols = ld_band.shape[1]
    blocks_here = ld_band.shape[0] // BLK
    span = band_cols + (1 << SHIFT_BITS) - 1
    padded = with_halo(vector, halo)
    need = (blocks_here - 1) * BLK + span
    padded = jnp.pad(padded, ((0, 0), (0, max(0, need - padded.shape[1]))))
    wide = jnp.stack([padded[:, b * BLK : b * BLK + span] for b in range(blocks_here)])
    for bit in range(SHIFT_BITS):
        step = 1 << bit
        take = (shifts >> bit & 1)[:, None, None] == 1
        wide = jnp.where(take, wide[:, :, step:], wide[:, :, :-step])
    windows = wide[:, :, :band_cols]
    blocks = ld_band.reshape(blocks_here, BLK, band_cols)
    product = jnp.einsum("btk,brk->tbr", windows, blocks, precision=lax.Precision.HIGHEST)
    return product.reshape(vector.shape) + ridge_shift[:, None] * vector


def local(beta_hat, ld_band, band_start, heritability, genotypes):
    n_snp = lax.axis_size("snp")
    n_ind = lax.axis_size("ind")
    n_all = n_snp * n_ind
    me_ind = lax.axis_index("ind")
    traits_here, rows_here = beta_hat.shape
    traits = traits_here * n_ind
    halo = ld_band.shape[1] - BLK - REACH
    offsets = band_start - lax.axis_index("snp") * rows_here + halo
    shifts = offsets - jnp.arange(band_start.shape[0], dtype=jnp.int32) * BLK
    ridge_shift = M_GENOME / N_GWAS / heritability
    colsum = jnp.sum(genotypes.astype(jnp.float32), axis=0)
    colsum = all_sum(colsum, "ind", n_ind)
    beta_all = lax.all_gather(beta_hat, "ind", axis=0, tiled=True)
    image = apply_operator(beta_hat, ld_band, shifts, ridge_shift, halo)
    image_all = lax.all_gather(image, "ind", axis=0, tiled=True)
    image2 = apply_operator(image, ld_band, shifts, ridge_shift, halo)
    moments = jnp.stack(
        [
            jnp.sum(beta_hat * beta_hat, axis=1),
            jnp.sum(beta_hat * image, axis=1),
            jnp.sum(image * image, axis=1),
            jnp.sum(image * image2, axis=1),
        ]
    )
    placed = jnp.zeros((4, traits), jnp.float32)
    placed = lax.dynamic_update_slice_in_dim(placed, moments, me_ind * traits_here, 1)
    m0, m1, m2, m3 = all_sum(placed, ("ind", "snp"), n_all)
    alpha1 = m0 / m1
    norm1 = alpha1 * alpha1 * m2 - m0
    ratio = norm1 / m0
    grow = 1.0 + ratio
    curv = grow * grow * m1 - 2.0 * grow * alpha1 * m2 + alpha1 * alpha1 * m3
    alpha2 = norm1 / curv
    residual = beta_all - alpha1[:, None] * image_all
    direction = residual + ratio[:, None] * beta_all
    weights_all = alpha1[:, None] * beta_all + alpha2[:, None] * direction
    weights = lax.dynamic_slice_in_dim(weights_all, me_ind * traits_here, traits_here, 0)
    rounded = weights_all.astype(jnp.bfloat16)
    partial = lax.dot_general(
        rounded, genotypes, (((1,), (1,)), ((), ())), preferred_element_type=jnp.float32
    )
    mean_part = jnp.sum(rounded.astype(jnp.float32) * colsum[None, :], axis=1)
    inds_here = genotypes.shape[0]
    share = inds_here // n_snp
    chunks = partial.reshape(traits, n_snp, share).transpose(1, 0, 2).reshape(n_snp, traits * share)
    extra = jnp.broadcast_to(
        jnp.pad(mean_part, (0, 128 - traits % 128 if traits % 128 else 0))[None],
        (n_snp, -(-traits // 128) * 128),
    )
    sent = jnp.concatenate([chunks, extra], axis=1).reshape(n_snp, -1, 128)
    got = jnp.sum(lax.all_to_all(sent, "snp", 0, 0, tiled=True), axis=0).reshape(-1)
    complete = got[: traits * share].reshape(traits, share)
    count = inds_here * n_ind
    average = got[traits * share : traits * share + traits] / count
    centred = complete - average[:, None]
    variance = all_sum(jnp.sum(centred * centred, axis=1), ("ind", "snp"), n_all) / count
    scores = centred * lax.rsqrt(variance + 1e-05)[:, None]
    return (weights, scores)


def solution(mesh):
    placed = (P("ind", "snp"), P("snp", None), P("snp"), P("ind"), P("ind", "snp"))
    return jax.shard_map(
        local,
        mesh=mesh,
        in_specs=placed,
        out_specs=(P("ind", "snp"), P(None, ("ind", "snp"))),
        check_vma=False,
    )
```

profile of v0, /device:TPU:0, one launch (start us, length us, event | category | flops | bytes accessed | tf_op | source)
XLA Modules:
  0.0 93.5 jit_solution(7003058788836734256)
XLA Ops:
  0.6 0.9 fusion.46
  1.5 4.9 %collective-permute-start = (f32[16,480]{1,0:T(8,128)S(1)}, f32[16,480]{1,0:T(8,128)S(1)}, u32[]{:S(2)}, u32[]{:S(2)}) collective-permute-start(f32[16,480]{1,0:T(8,128)S(1)} %get-tuple-element.16), channel_id=1, source_target_pairs={{0,4},{4,8},{8,12},{12,16},{16,20},{20,24},{24,28},{1,5},{5,9},{9,... | collective-permute-start | bytes 92168 | tf_op jit(solution)/shard_map/ppermute | solution.py:23
  6.4 1.3 %collective-permute-start.1 = (f32[16,480]{1,0:T(8,128)S(1)}, f32[16,480]{1,0:T(8,128)S(1)}, u32[]{:S(2)}, u32[]{:S(2)}) collective-permute-start(f32[16,480]{1,0:T(8,128)S(1)} %get-tuple-element.15), channel_id=1, source_target_pairs={{4,0},{8,4},{12,8},{16,12},{20,16},{24,20},{28,24},{5,1},{9,5},{13... | collective-permute-start | bytes 92168 | tf_op jit(solution)/shard_map/ppermute | solution.py:24
  7.7 2.0 %convert_reduce_fusion = f32[1024]{0:T(1024)S(1)} fusion(bf16[1024,1024]{1,0:T(8,128)(2,1)} %param.9), kind=kLoop, calls=%fused_computation | loop fusion | flops 2096128 | bytes 2101248 | tf_op jit(solution)/shard_map/reduce_sum | solution.py:57
  10.3 3.3 %all-to-all-start.1 = ((f32[4,1,1024]{2,1,0:T(1,128)}), f32[4,1,1024]{2,1,0:T(1,128)S(1)}, u32[]{:S(2)}, u32[]{:S(2)}) async-start(f32[4,1,1024]{2,1,0:T(1,128)} %broadcast_in_dim.136), calls=%async_computation.1 | async-start | bytes 32768 | tf_op jit(solution)/shard_map/all_to_all | solution.py:16
  13.5 0.7 and_compare_fusion.6
  14.2 0.7 broadcast_divide_fusion
  14.9 0.8 constant_dynamic-update-slice_fusion.1
  15.7 0.9 fusion.21
  16.6 0.9 fusion.18
  17.5 0.9 fusion.36
  18.4 0.9 %concatenate.30 = f32[16,1984]{1,0:T(8,128)S(1)} concatenate(f32[16,480]{1,0:T(8,128)S(1)} %collective-permute-done, f32[16,1024]{1,0:T(8,128)} %param.5, f32[16,480]{1,0:T(8,128)S(1)} %collective-permute-done.1), dimensions={1} | concatenate | bytes 253952 | tf_op jit(solution)/shard_map/concatenate | solution.py:25
  21.1 1.0 %copy-done = f32[1024,1024]{1,0:T(8,128)S(1)} copy-done((f32[1024,1024]{1,0:T(8,128)S(1)}, f32[1024,1024]{1,0:T(8,128)}, u32[]{:S(2)}) %copy-start) | copy-done | bytes 4194328
  22.1 3.7 %convolution_bitcast_fusion.2 = f32[8,2,8,128]{3,2,1,0:T(8,128)S(1)} fusion(f32[8,128,1024]{2,1,0:T(8,128)S(1)} %bitcast.133, f32[8,16,1088]{2,1,0:T(8,128)S(1)} %slice_select_fusion.6, pred[8]{0:T(512)(128)(4,1)S(1)} %get-tuple-element.11), kind=kOutput, calls=%fused_computation.3 | convolution fusion | flops 201457664 | bytes 5308928 | tf_op jit(solution)/shard_map/btk,brk->tbr/dot_general | solution.py:42
  25.9 4.5 %collective-permute-start.2 = (f32[16,480]{1,0:T(8,128)S(1)}, f32[16,480]{1,0:T(8,128)S(1)}, u32[]{:S(2)}, u32[]{:S(2)}) collective-permute-start(f32[16,480]{1,0:T(8,128)S(1)} %get-tuple-element.14), channel_id=1, source_target_pairs={{0,4},{4,8},{8,12},{12,16},{16,20},{20,24},{24,28},{1,5},{5,9},{9,... | collective-permute-start | bytes 92168 | tf_op jit(solution)/shard_map/ppermute | solution.py:23
  30.5 6.2 %all_gather.6 = f32[64,1024]{1,0:T(8,128)S(1)} all-gather(f32[16,1024]{1,0:T(8,128)S(1)} %copy-done.3), channel_id=1, replica_groups=mesh['snp'=8,'ind'=4] {'ind'}, dimensions={0}, use_global_device_ids=true | all-gather | bytes 327680 | tf_op jit(solution)/shard_map/all_gather | solution.py:59
  36.8 1.3 %collective-permute-start.3 = (f32[16,480]{1,0:T(8,128)S(1)}, f32[16,480]{1,0:T(8,128)S(1)}, u32[]{:S(2)}, u32[]{:S(2)}) collective-permute-start(f32[16,480]{1,0:T(8,128)S(1)} %get-tuple-element.13), channel_id=1, source_target_pairs={{4,0},{8,4},{12,8},{16,12},{20,16},{24,20},{28,24},{5,1},{9,5},{13... | collective-permute-start | bytes 92168 | tf_op jit(solution)/shard_map/ppermute | solution.py:24
  38.1 4.8 %collective-permute-done.3 = f32[16,480]{1,0:T(8,128)S(1)} collective-permute-done((f32[16,480]{1,0:T(8,128)S(1)}, f32[16,480]{1,0:T(8,128)S(1)}, u32[]{:S(2)}, u32[]{:S(2)}) %collective-permute-start.3) | collective-permute-done | bytes 30752 | tf_op jit(solution)/shard_map/ppermute | solution.py:24
  45.0 1.0 %copy-done.1 = f32[1024,1024]{1,0:T(8,128)S(1)} copy-done((f32[1024,1024]{1,0:T(8,128)S(1)}, f32[1024,1024]{1,0:T(8,128)}, u32[]{:S(2)}) %copy-start.1) | copy-done | bytes 4194328
  46.0 3.7 %convolution_bitcast_fusion.1 = f32[8,2,8,128]{3,2,1,0:T(8,128)S(1)} fusion(f32[8,128,1024]{2,1,0:T(8,128)S(1)} %bitcast.134, f32[8,16,1088]{2,1,0:T(8,128)S(1)} %slice_select_fusion, pred[8]{0:T(512)(128)(4,1)S(1)} %get-tuple-element.11), kind=kOutput, calls=%fused_computation.2 | convolution fusion | flops 201457664 | bytes 5308928 | tf_op jit(solution)/shard_map/btk,brk->tbr/dot_general | solution.py:42
  50.0 0.7 reshape.139
  50.8 6.4 %all-to-all-start = ((f32[32,1,256]{2,1,0:T(1,128)}), f32[32,1,256]{2,1,0:T(1,128)S(1)}, u32[]{:S(2)}, u32[]{:S(2)}) async-start(f32[32,1,256]{2,1,0:T(1,128)} %reshape.139), calls=%async_computation | async-start | bytes 65536 | tf_op jit(solution)/shard_map/all_to_all | solution.py:16
  57.1 6.1 %all_gather.7 = f32[64,1024]{1,0:T(8,128)S(1)} all-gather(f32[16,1024]{1,0:T(8,128)S(1)} %bitcast_add_fusion.1), channel_id=1, replica_groups=mesh['snp'=8,'ind'=4] {'ind'}, dimensions={0}, use_global_device_ids=true | all-gather | bytes 327680 | tf_op jit(solution)/shard_map/all_gather | solution.py:61
  63.3 1.0 %all-to-all-done = f32[32,1,256]{2,1,0:T(1,128)S(1)} async-done(((f32[32,1,256]{2,1,0:T(1,128)}), f32[32,1,256]{2,1,0:T(1,128)S(1)}, u32[]{:S(2)}, u32[]{:S(2)}) %all-to-all-start) | async-done | bytes 32800 | tf_op jit(solution)/shard_map/all_to_all | solution.py:16
  64.8 0.7 reduce.2
  66.0 0.8 convolution_bitcast_fusion
  66.9 15.1 %all_to_all.22 = f32[8,65,128]{2,1,0:T(8,128)S(1)} all-to-all(f32[8,65,128]{2,1,0:T(8,128)S(1)} %copy.21), channel_id=1, replica_groups=mesh['snp'=8,'ind'=4] {'snp'}, dimensions={0} | all-to-all | bytes 532480 | tf_op jit(solution)/shard_map/all_to_all | solution.py:97
  82.2 0.6 broadcast_in_dim.138
  82.8 2.9 %all-to-all-start.3 = ((f32[32,1,64]{2,1,0:T(1,128)}), f32[32,1,64]{2,1,0:T(1,128)S(1)}, u32[]{:S(2)}, u32[]{:S(2)}) async-start(f32[32,1,64]{2,1,0:T(1,128)} %broadcast_in_dim.138), calls=%async_computation.3 | async-start | bytes 32768 | tf_op jit(solution)/shard_map/all_to_all | solution.py:16
  85.7 0.6 constant_dynamic-slice_fusion
  86.3 6.4 %all-to-all-done.3 = f32[32,1,64]{2,1,0:T(1,128)S(1)} async-done(((f32[32,1,64]{2,1,0:T(1,128)}), f32[32,1,64]{2,1,0:T(1,128)S(1)}, u32[]{:S(2)}, u32[]{:S(2)}) %all-to-all-start.3) | async-done | bytes 8224 | tf_op jit(solution)/shard_map/all_to_all | solution.py:16
  92.8 0.7 fusion.40
  (61 shorter events, 6.1 us)
Async XLA Ops:
  1.5 14.2 %collective-permute-start = (f32[16,480]{1,0:T(8,128)S(1)}, f32[16,480]{1,0:T(8,128)S(1)}, u32[]{:S(2)}, u32[]{:S(2)}) collective-permute-start(f32[16,480]{1,0:T(8,128)S(1)} %get-tuple-element.16), channel_id=1, source_target_pairs={{0,4},{4,8},{8,12},{12,16},{16,20},{20,24},{24,28},{1,5},{5,9},{9,... | collective-permute-start | bytes 92168 | tf_op jit(solution)/shard_map/ppermute | solution.py:23
  6.4 12.0 %collective-permute-start.1 = (f32[16,480]{1,0:T(8,128)S(1)}, f32[16,480]{1,0:T(8,128)S(1)}, u32[]{:S(2)}, u32[]{:S(2)}) collective-permute-start(f32[16,480]{1,0:T(8,128)S(1)} %get-tuple-element.15), channel_id=1, source_target_pairs={{4,0},{8,4},{12,8},{16,12},{20,16},{24,20},{28,24},{5,1},{9,5},{13... | collective-permute-start | bytes 92168 | tf_op jit(solution)/shard_map/ppermute | solution.py:24
  10.3 26.5 %all-to-all-start.1 = ((f32[4,1,1024]{2,1,0:T(1,128)}), f32[4,1,1024]{2,1,0:T(1,128)S(1)}, u32[]{:S(2)}, u32[]{:S(2)}) async-start(f32[4,1,1024]{2,1,0:T(1,128)} %broadcast_in_dim.136), calls=%async_computation.1 | async-start | bytes 32768 | tf_op jit(solution)/shard_map/all_to_all | solution.py:16
  19.9 2.2 %copy-start = (f32[1024,1024]{1,0:T(8,128)S(1)}, f32[1024,1024]{1,0:T(8,128)}, u32[]{:S(2)}) copy-start(f32[1024,1024]{1,0:T(8,128)} %param.6) | copy-start | bytes 12582916
  20.6 5.1 %copy-start.3 = (f32[16,1024]{1,0:T(8,128)S(1)}, f32[16,1024]{1,0:T(8,128)}, u32[]{:S(2)}) copy-start(f32[16,1024]{1,0:T(8,128)} %param.5) | copy-start | bytes 196612
  25.9 12.1 %collective-permute-start.2 = (f32[16,480]{1,0:T(8,128)S(1)}, f32[16,480]{1,0:T(8,128)S(1)}, u32[]{:S(2)}, u32[]{:S(2)}) collective-permute-start(f32[16,480]{1,0:T(8,128)S(1)} %get-tuple-element.14), channel_id=1, source_target_pairs={{0,4},{4,8},{8,12},{12,16},{16,20},{20,24},{24,28},{1,5},{5,9},{9,... | collective-permute-start | bytes 92168 | tf_op jit(solution)/shard_map/ppermute | solution.py:23
  36.8 6.2 %collective-permute-start.3 = (f32[16,480]{1,0:T(8,128)S(1)}, f32[16,480]{1,0:T(8,128)S(1)}, u32[]{:S(2)}, u32[]{:S(2)}) collective-permute-start(f32[16,480]{1,0:T(8,128)S(1)} %get-tuple-element.13), channel_id=1, source_target_pairs={{4,0},{8,4},{12,8},{16,12},{20,16},{24,20},{28,24},{5,1},{9,5},{13... | collective-permute-start | bytes 92168 | tf_op jit(solution)/shard_map/ppermute | solution.py:24
  43.8 2.2 %copy-start.1 = (f32[1024,1024]{1,0:T(8,128)S(1)}, f32[1024,1024]{1,0:T(8,128)}, u32[]{:S(2)}) copy-start(f32[1024,1024]{1,0:T(8,128)} %param.6) | copy-start | bytes 12582916
  44.7 21.3 %copy-start.2 = (bf16[1024,1024]{1,0:T(8,128)(2,1)S(1)}, bf16[1024,1024]{1,0:T(8,128)(2,1)}, u32[]{:S(2)}) copy-start(bf16[1024,1024]{1,0:T(8,128)(2,1)} %param.9) | copy-start | bytes 6291460
  50.8 13.6 %all-to-all-start = ((f32[32,1,256]{2,1,0:T(1,128)}), f32[32,1,256]{2,1,0:T(1,128)S(1)}, u32[]{:S(2)}, u32[]{:S(2)}) async-start(f32[32,1,256]{2,1,0:T(1,128)} %reshape.139), calls=%async_computation | async-start | bytes 65536 | tf_op jit(solution)/shard_map/all_to_all | solution.py:16
  82.8 9.9 %all-to-all-start.3 = ((f32[32,1,64]{2,1,0:T(1,128)}), f32[32,1,64]{2,1,0:T(1,128)S(1)}, u32[]{:S(2)}, u32[]{:S(2)}) async-start(f32[32,1,64]{2,1,0:T(1,128)} %broadcast_in_dim.138), calls=%async_computation.3 | async-start | bytes 32768 | tf_op jit(solution)/shard_map/all_to_all | solution.py:16
where the time goes:
time: 94.3 us; the launch traced here: 93.5 us
  blocking collectives  27.4 us (29%)
  starting transfers between devices  24.5 us (26%)
  waiting for transfers between devices  12.3 us (13%)
  other arithmetic  11.5 us (12%)
  local copies, waits for them, and re-layouts  8.63 us (9%)
  matrix products  8.08 us (9%)
  between operations  1 us (1%)
    all_to_all x1, blocking collectives, local(): lax.all_to_all(sent, 'snp', 0, 0, tiled=True)  15.1 us
    all_to_all x3, starting transfers between devices, all_sum(): return jnp.sum(lax.all_to_all(sent, axes, 0, 0, tiled=True), axis=0)  12.5 us
    ppermute x2, starting transfers between devices, with_halo(): low = lax.ppermute(block[:, block.shape[1] - width:], 'snp', forward)  9.44 us
    all_to_all x3, waiting for transfers between devices, all_sum(): return jnp.sum(lax.all_to_all(sent, axes, 0, 0, tiled=True), axis=0)  7.48 us
    dot_general x2, matrix products, apply_operator(): jnp.einsum('btk,brk->tbr', windows, blocks, precision=lax.Precision.HIGHEST)  7.32 us
    all_gather x1, blocking collectives, local(): beta_all = lax.all_gather(beta_hat, 'ind', axis=0, tiled=True)  6.23 us
    all_gather x1, blocking collectives, local(): image_all = lax.all_gather(image, 'ind', axis=0, tiled=True)  6.14 us
    ppermute x2, waiting for transfers between devices, with_halo(): high = lax.ppermute(block[:, :width], 'snp', backward)  4.84 us
  transfers between devices with their start and end apart: 7, of which 3 were waited for; matrix products, arithmetic and copies ran while one was open for 16% of the time, Pallas kernels for 0%

commit v1 on v0

--- a/solution.py
+++ b/solution.py
@@ -56,9 +56,12 @@
     ridge_shift = M_GENOME / N_GWAS / heritability
     colsum = jnp.sum(genotypes.astype(jnp.float32), axis=0)
     colsum = all_sum(colsum, "ind", n_ind)
-    beta_all = lax.all_gather(beta_hat, "ind", axis=0, tiled=True)
     image = apply_operator(beta_hat, ld_band, shifts, ridge_shift, halo)
-    image_all = lax.all_gather(image, "ind", axis=0, tiled=True)
+    beta_all, image_all = jnp.split(
+        lax.all_gather(jnp.concatenate([beta_hat, image], axis=1), "ind", axis=0, tiled=True),
+        [beta_hat.shape[1]],
+        axis=1,
+    )
     image2 = apply_operator(image, ld_band, shifts, ridge_shift, halo)
     moments = jnp.stack(
         [

time: 94.3 us -> 89.7 us (0.951)
  blocking collectives: 27.4 us -> 23.6 us
  waiting for transfers between devices: 12.3 us -> 11.1 us
    all_gather x2 -> x1, blocking collectives: 12.4 us -> 7.69 us  [local(): lax.all_gather(jnp.concatenate([beta_hat, image], axis=1), 'ind', axis=0,...]
    all_to_all x3, starting transfers between devices: 12.5 us -> 13.8 us  [all_sum(): return jnp.sum(lax.all_to_all(sent, axes, 0, 0, tiled=True), axis=0)]
    all_to_all x3, waiting for transfers between devices: 7.48 us -> 6.43 us  [all_sum(): return jnp.sum(lax.all_to_all(sent, axes, 0, 0, tiled=True), axis=0)]
    ppermute x2, starting transfers between devices: 9.44 us -> 8.47 us  [with_halo(): low = lax.ppermute(block[:, block.shape[1] - width:], 'snp', forward)]
  transfers between devices with their start and end apart: 7 -> 7, of which waited for: 3 -> 3; matrix products, arithmetic and copies ran while one was open for 16% -> 7% of each run, Pallas kernels for 0% -> 0%
where the time goes in v1:
time: 89.7 us; the launch traced here: 88.9 us
  starting transfers between devices  24.9 us (28%)
  blocking collectives  23.6 us (26%)
  other arithmetic  11.5 us (13%)
  waiting for transfers between devices  11.1 us (12%)
  local copies, waits for them, and re-layouts  8.63 us (10%)
  matrix products  8.08 us (9%)
  between operations  1 us (1%)
    all_to_all x1, blocking collectives, local(): lax.all_to_all(sent, 'snp', 0, 0, tiled=True)  16 us
    all_to_all x3, starting transfers between devices, all_sum(): return jnp.sum(lax.all_to_all(sent, axes, 0, 0, tiled=True), axis=0)  13.8 us
    ppermute x2, starting transfers between devices, with_halo(): low = lax.ppermute(block[:, block.shape[1] - width:], 'snp', forward)  8.47 us
    all_gather x1, blocking collectives, local(): lax.all_gather(jnp.concatenate([beta_hat, image], axis=1), 'ind', axis=0,...  7.69 us
    dot_general x2, matrix products, apply_operator(): jnp.einsum('btk,brk->tbr', windows, blocks, precision=lax.Precision.HIGHEST)  7.32 us
    all_to_all x3, waiting for transfers between devices, all_sum(): return jnp.sum(lax.all_to_all(sent, axes, 0, 0, tiled=True), axis=0)  6.43 us
    ppermute x2, waiting for transfers between devices, with_halo(): high = lax.ppermute(block[:, :width], 'snp', backward)  4.42 us
    unnamed x17, local copies, waits for them, and re-layouts  4.02 us
  transfers between devices with their start and end apart: 7, of which 3 were waited for; matrix products, arithmetic and copies ran while one was open for 7% of the time, Pallas kernels for 0%

profile of v1, /device:TPU:0, one launch (start us, length us, event | category | flops | bytes accessed | tf_op | source)
XLA Modules:
  0.0 88.9 jit_solution(13754391755827849297)
XLA Ops:
  0.6 2.0 %convert_reduce_fusion = f32[1024]{0:T(1024)S(1)} fusion(bf16[1024,1024]{1,0:T(8,128)(2,1)} %param.9), kind=kLoop, calls=%fused_computation | loop fusion | flops 2096128 | bytes 2101248 | tf_op jit(solution)/shard_map/reduce_sum | solution.py:57
  2.6 0.6 broadcast_in_dim.136
  3.2 4.2 %all-to-all-start.1 = ((f32[4,1,1024]{2,1,0:T(1,128)}), f32[4,1,1024]{2,1,0:T(1,128)S(1)}, u32[]{:S(2)}, u32[]{:S(2)}) async-start(f32[4,1,1024]{2,1,0:T(1,128)} %broadcast_in_dim.136), calls=%async_computation.1 | async-start | bytes 32768 | tf_op jit(solution)/shard_map/all_to_all | solution.py:16
  7.4 0.8 fusion.51
  8.3 3.9 %collective-permute-start = (f32[16,480]{1,0:T(8,128)S(1)}, f32[16,480]{1,0:T(8,128)S(1)}, u32[]{:S(2)}, u32[]{:S(2)}) collective-permute-start(f32[16,480]{1,0:T(8,128)S(1)} %get-tuple-element.16), channel_id=1, source_target_pairs={{0,4},{4,8},{8,12},{12,16},{16,20},{20,24},{24,28},{1,5},{5,9},{9,... | collective-permute-start | bytes 92168 | tf_op jit(solution)/shard_map/ppermute | solution.py:23
  12.2 1.3 %collective-permute-start.1 = (f32[16,480]{1,0:T(8,128)S(1)}, f32[16,480]{1,0:T(8,128)S(1)}, u32[]{:S(2)}, u32[]{:S(2)}) collective-permute-start(f32[16,480]{1,0:T(8,128)S(1)} %get-tuple-element.15), channel_id=1, source_target_pairs={{4,0},{8,4},{12,8},{16,12},{20,16},{24,20},{28,24},{5,1},{9,5},{13... | collective-permute-start | bytes 92168 | tf_op jit(solution)/shard_map/ppermute | solution.py:24
  13.5 0.7 and_compare_fusion.6
  14.2 0.7 broadcast_divide_fusion
  14.9 0.8 constant_dynamic-update-slice_fusion.1
  15.8 0.9 fusion.25
  16.6 0.9 %fusion.22 = f32[8,16,1151]{2,1,0:T(8,128)S(1)} fusion(f32[8,16,1151]{2,1,0:T(8,128)S(1)} %fusion.25, f32[16,1024]{1,0:T(8,128)} %param.5, f32[16,480]{1,0:T(8,128)S(1)} %collective-permute-done), kind=kLoop, calls=%fused_computation.58 | loop fusion | flops 18416 | bytes 172032
  17.5 0.9 %fusion.40 = f32[8,16,1151]{2,1,0:T(8,128)S(1)} fusion(f32[8,16,1151]{2,1,0:T(8,128)S(1)} %fusion.22, f32[16,1024]{1,0:T(8,128)} %param.5, f32[16,480]{1,0:T(8,128)S(1)} %collective-permute-done), kind=kLoop, calls=%fused_computation.84 | loop fusion | flops 18416 | bytes 172032
  18.5 0.9 %concatenate.33 = f32[16,1984]{1,0:T(8,128)S(1)} concatenate(f32[16,480]{1,0:T(8,128)S(1)} %collective-permute-done, f32[16,1024]{1,0:T(8,128)} %param.5, f32[16,480]{1,0:T(8,128)S(1)} %collective-permute-done.1), dimensions={1} | concatenate | bytes 253952 | tf_op jit(solution)/shard_map/concatenate | solution.py:25
  21.1 1.0 %copy-done = f32[1024,1024]{1,0:T(8,128)S(1)} copy-done((f32[1024,1024]{1,0:T(8,128)S(1)}, f32[1024,1024]{1,0:T(8,128)}, u32[]{:S(2)}) %copy-start) | copy-done | bytes 4194328
  22.2 3.7 %convolution_bitcast_fusion.2 = f32[8,2,8,128]{3,2,1,0:T(8,128)S(1)} fusion(f32[8,128,1024]{2,1,0:T(8,128)S(1)} %bitcast.133, f32[8,16,1088]{2,1,0:T(8,128)S(1)} %slice_select_fusion.6, pred[8]{0:T(512)(128)(4,1)S(1)} %get-tuple-element.11), kind=kOutput, calls=%fused_computation.3 | convolution fusion | flops 201457664 | bytes 5308928 | tf_op jit(solution)/shard_map/btk,brk->tbr/dot_general | solution.py:42
  26.0 4.5 %collective-permute-start.2 = (f32[16,480]{1,0:T(8,128)S(1)}, f32[16,480]{1,0:T(8,128)S(1)}, u32[]{:S(2)}, u32[]{:S(2)}) collective-permute-start(f32[16,480]{1,0:T(8,128)S(1)} %get-tuple-element.14), channel_id=1, source_target_pairs={{0,4},{4,8},{8,12},{12,16},{16,20},{20,24},{24,28},{1,5},{5,9},{9,... | collective-permute-start | bytes 92168 | tf_op jit(solution)/shard_map/ppermute | solution.py:23
  30.5 1.3 %collective-permute-start.3 = (f32[16,480]{1,0:T(8,128)S(1)}, f32[16,480]{1,0:T(8,128)S(1)}, u32[]{:S(2)}, u32[]{:S(2)}) collective-permute-start(f32[16,480]{1,0:T(8,128)S(1)} %get-tuple-element.13), channel_id=1, source_target_pairs={{4,0},{8,4},{12,8},{16,12},{20,16},{24,20},{28,24},{5,1},{9,5},{13... | collective-permute-start | bytes 92168 | tf_op jit(solution)/shard_map/ppermute | solution.py:24
  32.4 4.4 %collective-permute-done.3 = f32[16,480]{1,0:T(8,128)S(1)} collective-permute-done((f32[16,480]{1,0:T(8,128)S(1)}, f32[16,480]{1,0:T(8,128)S(1)}, u32[]{:S(2)}, u32[]{:S(2)}) %collective-permute-start.3) | collective-permute-done | bytes 30752 | tf_op jit(solution)/shard_map/ppermute | solution.py:24
  38.6 1.0 %copy-done.1 = f32[1024,1024]{1,0:T(8,128)S(1)} copy-done((f32[1024,1024]{1,0:T(8,128)S(1)}, f32[1024,1024]{1,0:T(8,128)}, u32[]{:S(2)}) %copy-start.1) | copy-done | bytes 4194328
  39.6 3.7 %convolution_bitcast_fusion.1 = f32[8,2,8,128]{3,2,1,0:T(8,128)S(1)} fusion(f32[8,128,1024]{2,1,0:T(8,128)S(1)} %bitcast.134, f32[8,16,1088]{2,1,0:T(8,128)S(1)} %slice_select_fusion, pred[8]{0:T(512)(128)(4,1)S(1)} %get-tuple-element.11), kind=kOutput, calls=%fused_computation.2 | convolution fusion | flops 201457664 | bytes 5308928 | tf_op jit(solution)/shard_map/btk,brk->tbr/dot_general | solution.py:42
  43.7 0.7 reshape.139
  44.4 6.8 %all-to-all-start = ((f32[32,1,256]{2,1,0:T(1,128)}), f32[32,1,256]{2,1,0:T(1,128)S(1)}, u32[]{:S(2)}, u32[]{:S(2)}) async-start(f32[32,1,256]{2,1,0:T(1,128)} %reshape.139), calls=%async_computation | async-start | bytes 65536 | tf_op jit(solution)/shard_map/all_to_all | solution.py:16
  51.2 7.7 %all_gather.3 = f32[64,2048]{1,0:T(8,128)S(1)} all-gather(f32[16,2048]{1,0:T(8,128)S(1)} %pad_maximum_fusion), channel_id=1, replica_groups=mesh['snp'=8,'ind'=4] {'ind'}, dimensions={0}, use_global_device_ids=true | all-gather | bytes 655360 | tf_op jit(solution)/shard_map/all_gather | solution.py:61
  58.9 0.5 broadcast.122
  59.4 0.7 reduce.2
  60.6 0.8 convolution_bitcast_fusion
  61.5 16.0 %all_to_all.22 = f32[8,65,128]{2,1,0:T(8,128)S(1)} all-to-all(f32[8,65,128]{2,1,0:T(8,128)S(1)} %copy.21), channel_id=1, replica_groups=mesh['snp'=8,'ind'=4] {'snp'}, dimensions={0} | all-to-all | bytes 532480 | tf_op jit(solution)/shard_map/all_to_all | solution.py:100
  77.7 0.6 broadcast_in_dim.138
  78.3 2.8 %all-to-all-start.3 = ((f32[32,1,64]{2,1,0:T(1,128)}), f32[32,1,64]{2,1,0:T(1,128)S(1)}, u32[]{:S(2)}, u32[]{:S(2)}) async-start(f32[32,1,64]{2,1,0:T(1,128)} %broadcast_in_dim.138), calls=%async_computation.3 | async-start | bytes 32768 | tf_op jit(solution)/shard_map/all_to_all | solution.py:16
  81.1 0.6 constant_dynamic-slice_fusion
  81.7 6.4 %all-to-all-done.3 = f32[32,1,64]{2,1,0:T(1,128)S(1)} async-done(((f32[32,1,64]{2,1,0:T(1,128)}), f32[32,1,64]{2,1,0:T(1,128)S(1)}, u32[]{:S(2)}, u32[]{:S(2)}) %all-to-all-start.3) | async-done | bytes 8224 | tf_op jit(solution)/shard_map/all_to_all | solution.py:16
  88.2 0.7 fusion.44
  (61 shorter events, 5.2 us)
Async XLA Ops:
  3.2 12.5 %all-to-all-start.1 = ((f32[4,1,1024]{2,1,0:T(1,128)}), f32[4,1,1024]{2,1,0:T(1,128)S(1)}, u32[]{:S(2)}, u32[]{:S(2)}) async-start(f32[4,1,1024]{2,1,0:T(1,128)} %broadcast_in_dim.136), calls=%async_computation.1 | async-start | bytes 32768 | tf_op jit(solution)/shard_map/all_to_all | solution.py:16
  8.3 7.5 %collective-permute-start = (f32[16,480]{1,0:T(8,128)S(1)}, f32[16,480]{1,0:T(8,128)S(1)}, u32[]{:S(2)}, u32[]{:S(2)}) collective-permute-start(f32[16,480]{1,0:T(8,128)S(1)} %get-tuple-element.16), channel_id=1, source_target_pairs={{0,4},{4,8},{8,12},{12,16},{16,20},{20,24},{24,28},{1,5},{5,9},{9,... | collective-permute-start | bytes 92168 | tf_op jit(solution)/shard_map/ppermute | solution.py:23
  12.2 6.2 %collective-permute-start.1 = (f32[16,480]{1,0:T(8,128)S(1)}, f32[16,480]{1,0:T(8,128)S(1)}, u32[]{:S(2)}, u32[]{:S(2)}) collective-permute-start(f32[16,480]{1,0:T(8,128)S(1)} %get-tuple-element.15), channel_id=1, source_target_pairs={{4,0},{8,4},{12,8},{16,12},{20,16},{24,20},{28,24},{5,1},{9,5},{13... | collective-permute-start | bytes 92168 | tf_op jit(solution)/shard_map/ppermute | solution.py:24
  20.0 2.2 %copy-start = (f32[1024,1024]{1,0:T(8,128)S(1)}, f32[1024,1024]{1,0:T(8,128)}, u32[]{:S(2)}) copy-start(f32[1024,1024]{1,0:T(8,128)} %param.6) | copy-start | bytes 12582916
  20.7 5.1 %copy-start.3 = (f32[16,1024]{1,0:T(8,128)S(1)}, f32[16,1024]{1,0:T(8,128)}, u32[]{:S(2)}) copy-start(f32[16,1024]{1,0:T(8,128)} %param.5) | copy-start | bytes 196612
  26.0 6.1 %collective-permute-start.2 = (f32[16,480]{1,0:T(8,128)S(1)}, f32[16,480]{1,0:T(8,128)S(1)}, u32[]{:S(2)}, u32[]{:S(2)}) collective-permute-start(f32[16,480]{1,0:T(8,128)S(1)} %get-tuple-element.14), channel_id=1, source_target_pairs={{0,4},{4,8},{8,12},{12,16},{16,20},{20,24},{24,28},{1,5},{5,9},{9,... | collective-permute-start | bytes 92168 | tf_op jit(solution)/shard_map/ppermute | solution.py:23
  30.5 6.2 %collective-permute-start.3 = (f32[16,480]{1,0:T(8,128)S(1)}, f32[16,480]{1,0:T(8,128)S(1)}, u32[]{:S(2)}, u32[]{:S(2)}) collective-permute-start(f32[16,480]{1,0:T(8,128)S(1)} %get-tuple-element.13), channel_id=1, source_target_pairs={{4,0},{8,4},{12,8},{16,12},{20,16},{24,20},{28,24},{5,1},{9,5},{13... | collective-permute-start | bytes 92168 | tf_op jit(solution)/shard_map/ppermute | solution.py:24
  37.4 2.2 %copy-start.1 = (f32[1024,1024]{1,0:T(8,128)S(1)}, f32[1024,1024]{1,0:T(8,128)}, u32[]{:S(2)}) copy-start(f32[1024,1024]{1,0:T(8,128)} %param.6) | copy-start | bytes 12582916
  38.3 22.2 %copy-start.2 = (bf16[1024,1024]{1,0:T(8,128)(2,1)S(1)}, bf16[1024,1024]{1,0:T(8,128)(2,1)}, u32[]{:S(2)}) copy-start(bf16[1024,1024]{1,0:T(8,128)(2,1)} %param.9) | copy-start | bytes 6291460
  44.4 14.5 %all-to-all-start = ((f32[32,1,256]{2,1,0:T(1,128)}), f32[32,1,256]{2,1,0:T(1,128)S(1)}, u32[]{:S(2)}, u32[]{:S(2)}) async-start(f32[32,1,256]{2,1,0:T(1,128)} %reshape.139), calls=%async_computation | async-start | bytes 65536 | tf_op jit(solution)/shard_map/all_to_all | solution.py:16
  78.3 9.8 %all-to-all-start.3 = ((f32[32,1,64]{2,1,0:T(1,128)}), f32[32,1,64]{2,1,0:T(1,128)S(1)}, u32[]{:S(2)}, u32[]{:S(2)}) async-start(f32[32,1,64]{2,1,0:T(1,128)} %broadcast_in_dim.138), calls=%async_computation.3 | async-start | bytes 32768 | tf_op jit(solution)/shard_map/all_to_all | solution.py:16
